TPU v7x, 512 devices: a whole 4x8x8 slice. The times are simulated.
512 devices in a mesh: grp: 16 (over z, core), tok: 32 (over y, x).
Axes of the slice: x: 4, y: 8, z: 8, core: 2. Of those that a mesh axis runs over, the one named last changes fastest.
Arguments:
- patches: bfloat16 [32, 256, 1664], P('tok', 'grp'), may hold values from -54 to 54
- segment_ids: int32 [32, 256], P('tok'), may hold values from 0 to 32, as said below
- padding: int32 [32, 256], P('tok'), may hold values from 0 to 1, as said below
- request_owner: int32 [32, 32], P('tok'), may hold values from 0 to 31, as said below
- first_gain: float32 [1664], replicated, may hold values from 0.5 to 1.5
- first_shift: float32 [1664], replicated, may hold values from -3 to 3
- input_weight: bfloat16 [1664, 16, 312], P(None, 'grp'), may hold values from -0.15625 to 0.15625
- input_shift: float32 [16, 312], P('grp'), may hold values from -40 to 40
- output_weight: bfloat16 [16, 104, 1664], P('grp'), may hold values from -0.15625 to 0.15625
- output_shift: float32 [1664], replicated, may hold values from -3 to 3
- second_gain: float32 [1664], replicated, may hold values from 0.5 to 1.5
- second_shift: float32 [1664], replicated, may hold values from -3 to 3
- up_weight: bfloat16 [1664, 4096], P(None, 'grp'), may hold values from -0.15625 to 0.15625
- up_shift: float32 [4096], P('grp'), may hold values from -3 to 3
- down_weight: bfloat16 [4096, 1664], P('grp'), may hold values from -0.09375 to 0.09375
- down_shift: float32 [1664], replicated, may hold values from -3 to 3
- merge_weight: bfloat16 [6656, 1664], P(None, 'grp'), may hold values from -0.078125 to 0.078125
- merge_shift: float32 [1664], P('grp'), may hold values from -3 to 3
Outputs:
- routed: bfloat16 [32, 32, 8, 1664], P('tok', None, None, 'grp')
Inputs may be any that keep to these rules, and one draw needn't show every extreme that they name: `segment_ids`: patches come in aligned runs of four with one id (a 2x2 window); ids never fall along a group; an image spans 1 to 8 windows; every group holds an image of exactly 8 windows; padding stands at the end of a group and carries the id 32. `padding`: 0 exactly where segment_ids is 32. `request_owner`: every row is a permutation of 0 to 31; in every draw one owner receives an image of 8 windows from every group.
All inputs are finite; a program needn't handle non-finite values.
Results may differ from a plain program's by a relative error of at most 0.02.
The roundings to bfloat16 on the way count: a program that leaves them out, or rounds other values in their place, can miss the bound.
Values may be sent and summed in bfloat16 or wider, within the bound.
No kernel may reach another device: no remote copies, remote signals or barrier semaphores. Data moves between devices by JAX's collectives and lax.ppermute only.
A program may use at most 64 MiB of HBM per device.

v0:
```python
import jax
import jax.numpy as jnp
from jax import lax
from jax.sharding import PartitionSpec as P

CAP = 8
epsilon = 1e-06


def normalize(stream, factor, adjust):
    average = jnp.mean(stream, axis=-1, keepdims=True)
    centered = stream - average
    variance = jnp.mean(centered * centered, axis=-1, keepdims=True)
    return centered * lax.rsqrt(variance + epsilon) * factor + adjust


def attention_mask(segments, live_rows):
    count = segments.shape[0]
    same_image = segments[:, None] == segments[None, :]
    allowed = jnp.logical_and(same_image, live_rows[None, :] == 1)
    diagonal = jnp.arange(count)[:, None] == jnp.arange(count)[None, :]
    return jnp.logical_or(allowed, diagonal)


def softmax_rows(scores, allowed):
    masked = jnp.where(allowed, scores, -jnp.inf)
    row_max = jnp.max(masked, axis=-1, keepdims=True)
    powered = jnp.where(allowed, jnp.exp(masked - row_max), 0.0)
    return powered / jnp.sum(powered, axis=-1, keepdims=True)


def attend(projected, segments, live_rows, head_dim):
    queries = projected[:, :, :head_dim]
    key_rows = projected[:, :, head_dim : 2 * head_dim]
    value_rows = projected[:, :, 2 * head_dim :]
    scores = jnp.einsum(
        "qhe,khe->hqk", queries, key_rows, preferred_element_type=jnp.float32
    ) * head_dim ** (-0.5)
    probabilities = lax.optimization_barrier(
        softmax_rows(scores, attention_mask(segments, live_rows)[None]).astype(jnp.bfloat16)
    )
    return jnp.einsum(
        "hqk,khe->qhe", probabilities, value_rows, preferred_element_type=jnp.float32
    ).astype(jnp.bfloat16)


def summed_apart(terms):
    shards = lax.psum(1, "grp")
    rows = terms.shape[0] // shards
    pieces = lax.all_to_all(terms.reshape(shards, rows, terms.shape[1]), "grp", 0, 0, tiled=False)
    return jnp.sum(pieces.astype(jnp.float32), axis=0)


def routed_rows(merged, segments, live_rows, owners):
    window_segments = segments[::4]
    window_live = live_rows[::4]
    window_count = window_segments.shape[0]
    places = jnp.arange(window_count)
    earlier = jnp.logical_and(
        window_segments[None, :] == window_segments[:, None], places[None, :] < places[:, None]
    )
    slot_index = jnp.sum(earlier.astype(jnp.int32), axis=1)
    groups = owners.shape[0]
    matched = (jnp.arange(groups)[None, :] == window_segments[:, None]).astype(jnp.int32)
    owner_of = jnp.sum(matched * owners[None, :], axis=1)
    target = owner_of * CAP + slot_index
    one_hot = jnp.logical_and(
        target[:, None] == jnp.arange(groups * CAP)[None, :], window_live[:, None] == 1
    )
    outgoing = jnp.einsum(
        "wc,wd->cd", one_hot.astype(jnp.bfloat16), merged, preferred_element_type=jnp.float32
    )
    return outgoing.astype(jnp.bfloat16).reshape(groups, CAP, merged.shape[1])


def on_device(
    patches,
    segment_ids,
    padding,
    request_owner,
    first_gain,
    first_shift,
    input_weight,
    input_shift,
    output_weight,
    output_shift,
    second_gain,
    second_shift,
    up_weight,
    up_shift,
    down_weight,
    down_shift,
    merge_weight,
    merge_shift,
):
    row_count = patches.shape[1]
    model_width = patches.shape[2]
    head_dim = input_weight.shape[2] // 3
    segments = segment_ids[0]
    live_rows = padding[0]
    stream = patches[0]
    gathered = lax.all_gather(stream, "grp", axis=0, tiled=True)
    normed = normalize(gathered.astype(jnp.float32), first_gain, first_shift).astype(jnp.bfloat16)
    lifted = jnp.einsum("sd,dhe->she", normed, input_weight, preferred_element_type=jnp.float32)
    projected = (lifted + input_shift[None]).astype(jnp.bfloat16)
    mixed = attend(projected, segments, live_rows, head_dim)
    block = lax.optimization_barrier(mixed)
    attended = summed_apart(
        jnp.einsum("qhe,hed->qd", block, output_weight, preferred_element_type=jnp.float32).astype(
            jnp.bfloat16
        )
    )
    residual = (stream.astype(jnp.float32) + attended + output_shift).astype(jnp.bfloat16)
    normed_again = normalize(residual.astype(jnp.float32), second_gain, second_shift).astype(
        jnp.bfloat16
    )
    lifted = (
        jnp.dot(
            lax.all_gather(normed_again, "grp", axis=0, tiled=True),
            up_weight,
            preferred_element_type=jnp.float32,
        )
        + up_shift
    )
    activated = jax.nn.gelu(lifted, approximate=False).astype(jnp.bfloat16)
    block = lax.optimization_barrier(activated)
    fed = summed_apart(
        jnp.dot(block, down_weight, preferred_element_type=jnp.float32).astype(jnp.bfloat16)
    )
    layer_out = (residual.astype(jnp.float32) + fed + down_shift).astype(jnp.bfloat16)
    windows = layer_out.reshape(row_count // 4, 4 * model_width)
    merged = (
        jnp.dot(
            lax.all_gather(windows, "grp", axis=0, tiled=True),
            merge_weight,
            preferred_element_type=jnp.float32,
        )
        + merge_shift
    ).astype(jnp.bfloat16)
    outgoing = routed_rows(merged, segments, live_rows, request_owner[0])
    delivered = lax.all_to_all(outgoing, "tok", split_axis=0, concat_axis=0, tiled=True)
    return delivered[None]


def solution(mesh):
    return jax.shard_map(
        on_device,
        mesh=mesh,
        in_specs=(
            P("tok", "grp", None),
            P("tok", None),
            P("tok", None),
            P("tok", None),
            P(),
            P(),
            P(None, "grp", None),
            P("grp", None),
            P("grp", None, None),
            P(),
            P(),
            P(),
            P(None, "grp"),
            P("grp"),
            P("grp", None),
            P(),
            P(None, "grp"),
            P("grp"),
        ),
        out_specs=P("tok", None, None, "grp"),
        check_vma=False,
    )
```

profile of v0, /device:TPU:1, one launch (start us, length us, event | category | flops | bytes accessed | tf_op | source)
XLA Modules:
  0.0 143.6 jit_solution(7038068006779687679)
XLA Ops:
  0.0 27.2 %all-gather = bf16[1,256,1664]{2,1,0:T(8,128)(2,1)S(1)} all-gather(bf16[1,16,1664]{2,1,0:T(8,128)(2,1)} %param.18), channel_id=2, replica_groups=mesh['grp'=16,'tok'=32] {'grp'}, dimensions={1}, use_global_device_ids=true | all-gather | bytes 905216 | tf_op jit(solution)/shard_map/all_gather | solution.py:102
  27.2 0.2 convert_reduce_fusion
  27.5 0.4 fusion.3
  27.9 0.7 fusion.9
  28.6 0.3 fusion.50
  28.9 0.2 fusion.30
  29.2 0.2 fusion.10
  29.4 0.2 copy-done.3
  29.6 0.4 convolution_convert_fusion.1
  30.1 27.0 %all_to_all.15 = bf16[16,16,1664]{2,1,0:T(8,128)(2,1)S(1)} all-to-all(bf16[16,16,1664]{2,1,0:T(8,128)(2,1)S(1)} %bitcast.72), channel_id=1, replica_groups=mesh['grp'=16,'tok'=32] {'grp'}, dimensions={0} | all-to-all | bytes 1703936 | tf_op jit(solution)/shard_map/all_to_all | solution.py:50
  57.4 0.2 fusion.35
  57.7 16.8 %all_gather.10 = bf16[256,1664]{1,0:T(8,128)(2,1)S(1)} all-gather(bf16[16,1664]{1,0:T(8,128)(2,1)S(1)} %fusion.38), channel_id=1, replica_groups=mesh['grp'=16,'tok'=32] {'grp'}, dimensions={0}, use_global_device_ids=true | all-gather | bytes 905216 | tf_op jit(solution)/shard_map/all_gather | solution.py:119
  74.6 1.0 fusion.21
  75.6 0.2 copy-done.1
  75.7 1.4 convolution_convert_fusion
  77.1 5.3 %all-to-all-start.1 = ((bf16[16,16,1664]{2,1,0:T(8,128)(2,1)}), bf16[16,16,1664]{2,1,0:T(8,128)(2,1)S(1)}, u32[]{:S(2)}, u32[]{:S(2)}) async-start(bf16[16,16,1664]{2,1,0:T(8,128)(2,1)} %bitcast.17), calls=%async_computation.1 | async-start | bytes 1703936 | tf_op jit(solution)/shard_map/all_to_all | solution.py:50
  82.4 0.2 slice.15
  82.8 0.2 convert_reduce_fusion.4
  83.2 23.3 %all-to-all-done.1 = bf16[16,16,1664]{2,1,0:T(8,128)(2,1)S(1)} async-done(((bf16[16,16,1664]{2,1,0:T(8,128)(2,1)}), bf16[16,16,1664]{2,1,0:T(8,128)(2,1)S(1)}, u32[]{:S(2)}, u32[]{:S(2)}) %all-to-all-start.1) | async-done | bytes 852000 | tf_op jit(solution)/shard_map/all_to_all | solution.py:50
  106.7 16.8 %all-gather.1 = bf16[16,4,6656]{2,1,0:T(4,128)(2,1)S(1)} all-gather(bf16[1,4,6656]{2,1,0:T(4,128)(2,1)S(1)} %fusion.43), channel_id=1, replica_groups=mesh['grp'=16,'tok'=32] {'grp'}, dimensions={0}, use_global_device_ids=true | all-gather | bytes 905216 | tf_op jit(solution)/shard_map/all_gather | solution.py:134
  123.5 0.2 reshape.122
  123.7 0.8 convolution_convert_fusion.2
  124.7 18.3 %all_to_all.16 = bf16[32,8,104]{2,1,0:T(8,128)(2,1)S(1)} all-to-all(bf16[32,8,104]{2,1,0:T(8,128)(2,1)S(1)} %bitcast.73), channel_id=1, replica_groups=mesh['grp'=16,'tok'=32] {'tok'}, dimensions={0} | all-to-all | bytes 106496 | tf_op jit(solution)/shard_map/all_to_all | solution.py:141
  143.0 0.6 copy.29
  (58 shorter events, 1.4 us)
Async XLA Ops:
  0.0 123.7 %copy-start = (bf16[6656,104]{0,1:T(8,128)(2,1)S(1)}, bf16[6656,104]{0,1:T(8,128)(2,1)}, u32[]{:S(2)}) copy-start(bf16[6656,104]{0,1:T(8,128)(2,1)} %param.34) | copy-start | bytes 4153348
  0.0 27.8 %copy-start.16 = (s32[1,256]{1,0:T(1,128)S(1)}, s32[1,256]{1,0:T(1,128)}, u32[]{:S(2)}) copy-start(s32[1,256]{1,0:T(1,128)} %param.20) | copy-start | bytes 3076
  0.0 27.9 %copy-start.9 = (f32[1,312]{1,0:T(1,128)S(1)}, f32[1,312]{1,0:T(1,128)}, u32[]{:S(2)}) copy-start(f32[1,312]{1,0:T(1,128)} %param.25) | copy-start | bytes 3748
  0.0 27.9 %copy-start.14 = (f32[1664]{0:T(1024)S(1)}, f32[1664]{0:T(1024)}, u32[]{:S(2)}) copy-start(f32[1664]{0:T(1024)} %param.22) | copy-start | bytes 19972
  0.0 27.9 %copy-start.13 = (f32[1664]{0:T(1024)S(1)}, f32[1664]{0:T(1024)}, u32[]{:S(2)}) copy-start(f32[1664]{0:T(1024)} %param.23) | copy-start | bytes 19972
  0.0 27.9 %copy-start.11 = (bf16[1664,1,312]{0,2,1:T(8,128)(2,1)S(1)}, bf16[1664,1,312]{0,2,1:T(8,128)(2,1)}, u32[]{:S(2)}) copy-start(bf16[1664,1,312]{0,2,1:T(8,128)(2,1)} %param.24) | copy-start | bytes 3115012
  27.9 0.7 copy-start.5
  28.6 1.0 copy-start.3
  30.0 27.2 %copy-start.2 = (bf16[1,16,1664]{2,1,0:T(8,128)(2,1)S(1)}, bf16[1,16,1664]{2,1,0:T(8,128)(2,1)}, u32[]{:S(2)}) copy-start(bf16[1,16,1664]{2,1,0:T(8,128)(2,1)} %param.18) | copy-start | bytes 159748
  30.1 27.2 %copy-start.4 = (f32[1664]{0:T(1024)S(1)}, f32[1664]{0:T(1024)}, u32[]{:S(2)}) copy-start(f32[1664]{0:T(1024)} %param.27) | copy-start | bytes 19972
  30.1 27.6 %copy-start.7 = (f32[1664]{0:T(1024)S(1)}, f32[1664]{0:T(1024)}, u32[]{:S(2)}) copy-start(f32[1664]{0:T(1024)} %param.29) | copy-start | bytes 19972
  30.1 27.6 %copy-start.8 = (f32[1664]{0:T(1024)S(1)}, f32[1664]{0:T(1024)}, u32[]{:S(2)}) copy-start(f32[1664]{0:T(1024)} %param.28) | copy-start | bytes 19972
  57.1 17.4 %copy-start.12 = (bf16[1664,256]{1,0:T(8,128)(2,1)S(1)}, bf16[1664,256]{1,0:T(8,128)(2,1)}, u32[]{:S(2)}) copy-start(bf16[1664,256]{1,0:T(8,128)(2,1)} %param.30) | copy-start | bytes 2555908
  57.1 17.4 %copy-start.15 = (f32[256]{0:T(256)S(1)}, f32[256]{0:T(256)}, u32[]{:S(2)}) copy-start(f32[256]{0:T(256)} %param.31) | copy-start | bytes 3076
  74.6 1.2 copy-start.1
  77.1 5.6 %copy-start.6 = (f32[1664]{0:T(1024)S(1)}, f32[1664]{0:T(1024)}, u32[]{:S(2)}) copy-start(f32[1664]{0:T(1024)} %param.33) | copy-start | bytes 19972
  77.1 5.9 %copy-start.17 = (s32[1,32]{1,0:T(1,128)S(1)}, s32[1,32]{1,0:T(1,128)}, u32[]{:S(2)}) copy-start(s32[1,32]{1,0:T(1,128)} %param.21) | copy-start | bytes 388
  77.1 29.4 %all-to-all-start.1 = ((bf16[16,16,1664]{2,1,0:T(8,128)(2,1)}), bf16[16,16,1664]{2,1,0:T(8,128)(2,1)S(1)}, u32[]{:S(2)}, u32[]{:S(2)}) async-start(bf16[16,16,1664]{2,1,0:T(8,128)(2,1)} %bitcast.17), calls=%async_computation.1 | async-start | bytes 1703936 | tf_op jit(solution)/shard_map/all_to_all | solution.py:50
  106.7 17.0 %copy-start.10 = (f32[104]{0:T(128)S(1)}, f32[104]{0:T(128)}, u32[]{:S(2)}) copy-start(f32[104]{0:T(128)} %param.35) | copy-start | bytes 1252
where the time goes:
time: 144 us
  blocking collectives  106 us (74%)
  waiting for transfers between devices  23.3 us (16%)
  starting transfers between devices  5.33 us (4%)
  matrix products  4.68 us (3%)
  other arithmetic  1.96 us (1%)
  local copies, waits for them, and re-layouts  1.85 us (1%)
    all_gather x1, blocking collectives, on_device(): gathered = lax.all_gather(stream, 'grp', axis=0, tiled=True)  27.2 us
    all_to_all x1, blocking collectives, summed_apart(): lax.all_to_all(terms.reshape(shards, rows, terms.shape[1]), 'grp', 0, 0,...  27 us
    all_to_all x1, waiting for transfers between devices, summed_apart(): lax.all_to_all(terms.reshape(shards, rows, terms.shape[1]), 'grp', 0, 0,...  23.3 us
    all_to_all x1, blocking collectives, on_device(): lax.all_to_all(outgoing, 'tok', split_axis=0, concat_axis=0, tiled=True)  18.3 us
    all_gather x1, blocking collectives, on_device(): lax.all_gather(windows, 'grp', axis=0, tiled=True)  16.8 us
    all_gather x1, blocking collectives, on_device(): lax.all_gather(normed_again, 'grp', axis=0, tiled=True)  16.8 us
    all_to_all x1, starting transfers between devices, summed_apart(): lax.all_to_all(terms.reshape(shards, rows, terms.shape[1]), 'grp', 0, 0,...  5.33 us
  transfers between devices with their start and end apart: 1, of which 1 were waited for; matrix products, arithmetic and copies ran while one was open for 0% of the time, Pallas kernels for 0%

commit v1 on v0

--- a/solution.py
+++ b/solution.py
@@ -99,7 +99,16 @@
     segments = segment_ids[0]
     live_rows = padding[0]
     stream = patches[0]
-    gathered = lax.all_gather(stream, "grp", axis=0, tiled=True)
+    ways = lax.axis_size("grp")
+    up = [(d, (d + 1) % ways) for d in range(ways)]
+    down = [(d, (d - 1) % ways) for d in range(ways)]
+    earlier_2, later = ([stream], [stream])
+    for _ in range(ways // 2):
+        earlier_2.append(lax.ppermute(earlier_2[-1], "grp", up))
+    for _ in range((ways - 1) // 2):
+        later.append(lax.ppermute(later[-1], "grp", down))
+    line = jnp.concatenate([*earlier_2[::-1], *later[1:]], axis=0)
+    gathered = jnp.roll(line, (lax.axis_index("grp") - ways // 2) * stream.shape[0], axis=0)
     normed = normalize(gathered.astype(jnp.float32), first_gain, first_shift).astype(jnp.bfloat16)
     lifted = jnp.einsum("sd,dhe->she", normed, input_weight, preferred_element_type=jnp.float32)
     projected = (lifted + input_shift[None]).astype(jnp.bfloat16)

time: 144 us -> 166 us (1.15)
  starting transfers between devices: 5.33 us -> 36.4 us
  blocking collectives: 106 us -> 84.9 us
  waiting for transfers between devices: 23.3 us -> 32.7 us
    ppermute x0 -> x15, starting transfers between devices: none -> 31.2 us  [the longest x7 27.7 us: on_device(): later.append(lax.ppermute(later[-1], 'grp', down))]
    all_gather x1 -> x0, blocking collectives: 27.2 us -> none  [on_device(): gathered = lax.all_gather(stream, 'grp', axis=0, tiled=True)]
    ppermute x0 -> x15, waiting for transfers between devices: none -> 9.48 us  [the longest x8 7.64 us: on_device(): earlier_2.append(lax.ppermute(earlier_2[-1], 'grp', up))]
    all_to_all x1, blocking collectives: 27 us -> 32.9 us  [summed_apart(): lax.all_to_all(terms.reshape(shards, rows, terms.shape[1]), 'grp', 0, 0,...]
  transfers between devices with their start and end apart: 1 -> 16, of which waited for: 1 -> 13; matrix products, arithmetic and copies ran while one was open for 0% -> 2% of each run, Pallas kernels for 0% -> 0%
where the time goes in v1:
time: 166 us
  blocking collectives  84.9 us (51%)
  starting transfers between devices  36.4 us (22%)
  waiting for transfers between devices  32.7 us (20%)
  matrix products  4.66 us (3%)
  local copies, waits for them, and re-layouts  3.37 us (2%)
  other arithmetic  3.32 us (2%)
    all_to_all x1, blocking collectives, summed_apart(): lax.all_to_all(terms.reshape(shards, rows, terms.shape[1]), 'grp', 0, 0,...  32.9 us
    ppermute x7, starting transfers between devices, on_device(): later.append(lax.ppermute(later[-1], 'grp', down))  27.7 us
    all_to_all x1, waiting for transfers between devices, summed_apart(): lax.all_to_all(terms.reshape(shards, rows, terms.shape[1]), 'grp', 0, 0,...  23.3 us
    all_to_all x1, blocking collectives, on_device(): lax.all_to_all(outgoing, 'tok', split_axis=0, concat_axis=0, tiled=True)  18.3 us
    all_gather x1, blocking collectives, on_device(): lax.all_gather(windows, 'grp', axis=0, tiled=True)  16.8 us
    all_gather x1, blocking collectives, on_device(): lax.all_gather(normed_again, 'grp', axis=0, tiled=True)  16.8 us
    ppermute x8, waiting for transfers between devices, on_device(): earlier_2.append(lax.ppermute(earlier_2[-1], 'grp', up))  7.64 us
    all_to_all x1, starting transfers between devices, summed_apart(): lax.all_to_all(terms.reshape(shards, rows, terms.shape[1]), 'grp', 0, 0,...  5.2 us
  transfers between devices with their start and end apart: 16, of which 13 were waited for; matrix products, arithmetic and copies ran while one was open for 2% of the time, Pallas kernels for 0%

profile of v1, /device:TPU:1, one launch (start us, length us, event | category | flops | bytes accessed | tf_op | source)
XLA Modules:
  0.0 165.8 jit_solution(6201732892548366074)
XLA Ops:
  0.0 3.5 %collective-permute-start = (bf16[16,1664]{1,0:T(8,128)(2,1)}, bf16[16,1664]{1,0:T(8,128)(2,1)S(1)}, u32[]{:S(2)}, u32[]{:S(2)}) collective-permute-start(bf16[16,1664]{1,0:T(8,128)(2,1)} %bitcast.54), channel_id=1, source_target_pairs={{0,32},{32,64},{64,96},{96,128},{128,160},{160,192},{192,224},{224... | collective-permute-start | bytes 159752 | tf_op jit(solution)/shard_map/ppermute | solution.py:107
  3.5 4.3 %collective-permute-done = bf16[16,1664]{1,0:T(8,128)(2,1)S(1)} collective-permute-done((bf16[16,1664]{1,0:T(8,128)(2,1)}, bf16[16,1664]{1,0:T(8,128)(2,1)S(1)}, u32[]{:S(2)}, u32[]{:S(2)}) %collective-permute-start) | collective-permute-done | bytes 53280 | tf_op jit(solution)/shard_map/ppermute | solution.py:107
  7.8 4.3 %collective-permute-start.8 = (bf16[16,1664]{1,0:T(8,128)(2,1)}, bf16[16,1664]{1,0:T(8,128)(2,1)S(1)}, u32[]{:S(2)}, u32[]{:S(2)}) collective-permute-start(bf16[16,1664]{1,0:T(8,128)(2,1)} %bitcast.55), channel_id=1, source_target_pairs={{0,480},{32,0},{64,32},{96,64},{128,96},{160,128},{192,160},{224,1... | collective-permute-start | bytes 159752 | tf_op jit(solution)/shard_map/ppermute | solution.py:109
  12.0 0.7 collective-permute-done.1
  13.1 4.0 %collective-permute-start.9 = (bf16[16,1664]{1,0:T(8,128)(2,1)S(1)}, bf16[16,1664]{1,0:T(8,128)(2,1)S(1)}, u32[]{:S(2)}, u32[]{:S(2)}) collective-permute-start(bf16[16,1664]{1,0:T(8,128)(2,1)S(1)} %collective-permute-done.8), channel_id=1, source_target_pairs={{0,480},{32,0},{64,32},{96,64},{128,96},{160,128},{192,160},{224,1... | collective-permute-start | bytes 159752 | tf_op jit(solution)/shard_map/ppermute | solution.py:109
  18.0 3.8 %collective-permute-start.10 = (bf16[16,1664]{1,0:T(8,128)(2,1)S(1)}, bf16[16,1664]{1,0:T(8,128)(2,1)S(1)}, u32[]{:S(2)}, u32[]{:S(2)}) collective-permute-start(bf16[16,1664]{1,0:T(8,128)(2,1)S(1)} %collective-permute-done.9), channel_id=1, source_target_pairs={{0,480},{32,0},{64,32},{96,64},{128,96},{160,128},{192,160},{224,1... | collective-permute-start | bytes 159752 | tf_op jit(solution)/shard_map/ppermute | solution.py:109
  22.7 3.9 %collective-permute-start.11 = (bf16[16,1664]{1,0:T(8,128)(2,1)S(1)}, bf16[16,1664]{1,0:T(8,128)(2,1)S(1)}, u32[]{:S(2)}, u32[]{:S(2)}) collective-permute-start(bf16[16,1664]{1,0:T(8,128)(2,1)S(1)} %collective-permute-done.10), channel_id=1, source_target_pairs={{0,480},{32,0},{64,32},{96,64},{128,96},{160,128},{192,160},{224,1... | collective-permute-start | bytes 159752 | tf_op jit(solution)/shard_map/ppermute | solution.py:109
  27.4 3.9 %collective-permute-start.12 = (bf16[16,1664]{1,0:T(8,128)(2,1)S(1)}, bf16[16,1664]{1,0:T(8,128)(2,1)S(1)}, u32[]{:S(2)}, u32[]{:S(2)}) collective-permute-start(bf16[16,1664]{1,0:T(8,128)(2,1)S(1)} %collective-permute-done.11), channel_id=1, source_target_pairs={{0,480},{32,0},{64,32},{96,64},{128,96},{160,128},{192,160},{224,1... | collective-permute-start | bytes 159752 | tf_op jit(solution)/shard_map/ppermute | solution.py:109
  32.2 3.9 %collective-permute-start.13 = (bf16[16,1664]{1,0:T(8,128)(2,1)S(1)}, bf16[16,1664]{1,0:T(8,128)(2,1)S(1)}, u32[]{:S(2)}, u32[]{:S(2)}) collective-permute-start(bf16[16,1664]{1,0:T(8,128)(2,1)S(1)} %collective-permute-done.12), channel_id=1, source_target_pairs={{0,480},{32,0},{64,32},{96,64},{128,96},{160,128},{192,160},{224,1... | collective-permute-start | bytes 159752 | tf_op jit(solution)/shard_map/ppermute | solution.py:109
  36.6 0.7 compare_reduce_fusion
  37.3 0.7 reduce.4
  38.1 4.1 %collective-permute-start.14 = (bf16[16,1664]{1,0:T(8,128)(2,1)S(1)}, bf16[16,1664]{1,0:T(8,128)(2,1)S(1)}, u32[]{:S(2)}, u32[]{:S(2)}) collective-permute-start(bf16[16,1664]{1,0:T(8,128)(2,1)S(1)} %collective-permute-done.13), channel_id=1, source_target_pairs={{0,480},{32,0},{64,32},{96,64},{128,96},{160,128},{192,160},{224,1... | collective-permute-start | bytes 159752 | tf_op jit(solution)/shard_map/ppermute | solution.py:109
  42.2 0.8 constant_dynamic-update-slice_fusion.23
  44.4 0.7 fusion.8
  46.5 32.9 %all_to_all.15 = bf16[16,16,1664]{2,1,0:T(8,128)(2,1)S(1)} all-to-all(bf16[16,16,1664]{2,1,0:T(8,128)(2,1)S(1)} %bitcast.53), channel_id=1, replica_groups=mesh['grp'=16,'tok'=32] {'grp'}, dimensions={0} | all-to-all | bytes 1703936 | tf_op jit(solution)/shard_map/all_to_all | solution.py:50
  80.0 16.8 %all_gather.6 = bf16[256,1664]{1,0:T(8,128)(2,1)S(1)} all-gather(bf16[16,1664]{1,0:T(8,128)(2,1)S(1)} %fusion.38), channel_id=1, replica_groups=mesh['grp'=16,'tok'=32] {'grp'}, dimensions={0}, use_global_device_ids=true | all-gather | bytes 905216 | tf_op jit(solution)/shard_map/all_gather | solution.py:128
  96.8 1.0 fusion.21
  98.0 1.3 convolution_convert_fusion
  99.3 5.2 %all-to-all-start.1 = ((bf16[16,16,1664]{2,1,0:T(8,128)(2,1)}), bf16[16,16,1664]{2,1,0:T(8,128)(2,1)S(1)}, u32[]{:S(2)}, u32[]{:S(2)}) async-start(bf16[16,16,1664]{2,1,0:T(8,128)(2,1)} %bitcast.16), calls=%async_computation.1 | async-start | bytes 1703936 | tf_op jit(solution)/shard_map/all_to_all | solution.py:50
  105.3 23.3 %all-to-all-done.1 = bf16[16,16,1664]{2,1,0:T(8,128)(2,1)S(1)} async-done(((bf16[16,16,1664]{2,1,0:T(8,128)(2,1)}), bf16[16,16,1664]{2,1,0:T(8,128)(2,1)S(1)}, u32[]{:S(2)}, u32[]{:S(2)}) %all-to-all-start.1) | async-done | bytes 852000 | tf_op jit(solution)/shard_map/all_to_all | solution.py:50
  128.8 16.8 %all-gather = bf16[16,4,6656]{2,1,0:T(4,128)(2,1)S(1)} all-gather(bf16[1,4,6656]{2,1,0:T(4,128)(2,1)S(1)} %fusion.41), channel_id=1, replica_groups=mesh['grp'=16,'tok'=32] {'grp'}, dimensions={0}, use_global_device_ids=true | all-gather | bytes 905216 | tf_op jit(solution)/shard_map/all_gather | solution.py:143
  145.9 0.8 convolution_convert_fusion.2
  146.8 18.3 %all_to_all.16 = bf16[32,8,104]{2,1,0:T(8,128)(2,1)S(1)} all-to-all(bf16[32,8,104]{2,1,0:T(8,128)(2,1)S(1)} %bitcast.56), channel_id=1, replica_groups=mesh['grp'=16,'tok'=32] {'tok'}, dimensions={0} | all-to-all | bytes 106496 | tf_op jit(solution)/shard_map/all_to_all | solution.py:150
  165.1 0.6 copy.60
  (117 shorter events, 9.2 us)
Async XLA Ops:
  0.0 145.9 %copy-start = (bf16[6656,104]{0,1:T(8,128)(2,1)S(1)}, bf16[6656,104]{0,1:T(8,128)(2,1)}, u32[]{:S(2)}) copy-start(bf16[6656,104]{0,1:T(8,128)(2,1)} %param.34) | copy-start | bytes 4153348
  0.0 43.3 %copy-start.2 = (bf16[1,16,1664]{2,1,0:T(8,128)(2,1)S(1)}, bf16[1,16,1664]{2,1,0:T(8,128)(2,1)}, u32[]{:S(2)}) copy-start(bf16[1,16,1664]{2,1,0:T(8,128)(2,1)} %param.18) | copy-start | bytes 159748
  0.0 7.8 %collective-permute-start = (bf16[16,1664]{1,0:T(8,128)(2,1)}, bf16[16,1664]{1,0:T(8,128)(2,1)S(1)}, u32[]{:S(2)}, u32[]{:S(2)}) collective-permute-start(bf16[16,1664]{1,0:T(8,128)(2,1)} %bitcast.54), channel_id=1, source_target_pairs={{0,32},{32,64},{64,96},{96,128},{128,160},{160,192},{192,224},{224... | collective-permute-start | bytes 159752 | tf_op jit(solution)/shard_map/ppermute | solution.py:107
  7.8 5.0 %collective-permute-start.1 = (bf16[16,1664]{1,0:T(8,128)(2,1)S(1)}, bf16[16,1664]{1,0:T(8,128)(2,1)S(1)}, u32[]{:S(2)}, u32[]{:S(2)}) collective-permute-start(bf16[16,1664]{1,0:T(8,128)(2,1)S(1)} %collective-permute-done), channel_id=1, source_target_pairs={{0,32},{32,64},{64,96},{96,128},{128,160},{160,192},{192,224},{224... | collective-permute-start | bytes 159752 | tf_op jit(solution)/shard_map/ppermute | solution.py:107
  7.8 5.4 %collective-permute-start.8 = (bf16[16,1664]{1,0:T(8,128)(2,1)}, bf16[16,1664]{1,0:T(8,128)(2,1)S(1)}, u32[]{:S(2)}, u32[]{:S(2)}) collective-permute-start(bf16[16,1664]{1,0:T(8,128)(2,1)} %bitcast.55), channel_id=1, source_target_pairs={{0,480},{32,0},{64,32},{96,64},{128,96},{160,128},{192,160},{224,1... | collective-permute-start | bytes 159752 | tf_op jit(solution)/shard_map/ppermute | solution.py:109
  12.8 4.8 %collective-permute-start.2 = (bf16[16,1664]{1,0:T(8,128)(2,1)S(1)}, bf16[16,1664]{1,0:T(8,128)(2,1)S(1)}, u32[]{:S(2)}, u32[]{:S(2)}) collective-permute-start(bf16[16,1664]{1,0:T(8,128)(2,1)S(1)} %collective-permute-done.1), channel_id=1, source_target_pairs={{0,32},{32,64},{64,96},{96,128},{128,160},{160,192},{192,224},{224... | collective-permute-start | bytes 159752 | tf_op jit(solution)/shard_map/ppermute | solution.py:107
  13.1 4.8 %collective-permute-start.9 = (bf16[16,1664]{1,0:T(8,128)(2,1)S(1)}, bf16[16,1664]{1,0:T(8,128)(2,1)S(1)}, u32[]{:S(2)}, u32[]{:S(2)}) collective-permute-start(bf16[16,1664]{1,0:T(8,128)(2,1)S(1)} %collective-permute-done.8), channel_id=1, source_target_pairs={{0,480},{32,0},{64,32},{96,64},{128,96},{160,128},{192,160},{224,1... | collective-permute-start | bytes 159752 | tf_op jit(solution)/shard_map/ppermute | solution.py:109
  17.5 4.8 %collective-permute-start.3 = (bf16[16,1664]{1,0:T(8,128)(2,1)S(1)}, bf16[16,1664]{1,0:T(8,128)(2,1)S(1)}, u32[]{:S(2)}, u32[]{:S(2)}) collective-permute-start(bf16[16,1664]{1,0:T(8,128)(2,1)S(1)} %collective-permute-done.2), channel_id=1, source_target_pairs={{0,32},{32,64},{64,96},{96,128},{128,160},{160,192},{192,224},{224... | collective-permute-start | bytes 159752 | tf_op jit(solution)/shard_map/ppermute | solution.py:107
  18.0 4.7 %collective-permute-start.10 = (bf16[16,1664]{1,0:T(8,128)(2,1)S(1)}, bf16[16,1664]{1,0:T(8,128)(2,1)S(1)}, u32[]{:S(2)}, u32[]{:S(2)}) collective-permute-start(bf16[16,1664]{1,0:T(8,128)(2,1)S(1)} %collective-permute-done.9), channel_id=1, source_target_pairs={{0,480},{32,0},{64,32},{96,64},{128,96},{160,128},{192,160},{224,1... | collective-permute-start | bytes 159752 | tf_op jit(solution)/shard_map/ppermute | solution.py:109
  22.3 4.8 %collective-permute-start.4 = (bf16[16,1664]{1,0:T(8,128)(2,1)S(1)}, bf16[16,1664]{1,0:T(8,128)(2,1)S(1)}, u32[]{:S(2)}, u32[]{:S(2)}) collective-permute-start(bf16[16,1664]{1,0:T(8,128)(2,1)S(1)} %collective-permute-done.3), channel_id=1, source_target_pairs={{0,32},{32,64},{64,96},{96,128},{128,160},{160,192},{192,224},{224... | collective-permute-start | bytes 159752 | tf_op jit(solution)/shard_map/ppermute | solution.py:107
  22.7 4.8 %collective-permute-start.11 = (bf16[16,1664]{1,0:T(8,128)(2,1)S(1)}, bf16[16,1664]{1,0:T(8,128)(2,1)S(1)}, u32[]{:S(2)}, u32[]{:S(2)}) collective-permute-start(bf16[16,1664]{1,0:T(8,128)(2,1)S(1)} %collective-permute-done.10), channel_id=1, source_target_pairs={{0,480},{32,0},{64,32},{96,64},{128,96},{160,128},{192,160},{224,1... | collective-permute-start | bytes 159752 | tf_op jit(solution)/shard_map/ppermute | solution.py:109
  27.1 4.8 %collective-permute-start.5 = (bf16[16,1664]{1,0:T(8,128)(2,1)S(1)}, bf16[16,1664]{1,0:T(8,128)(2,1)S(1)}, u32[]{:S(2)}, u32[]{:S(2)}) collective-permute-start(bf16[16,1664]{1,0:T(8,128)(2,1)S(1)} %collective-permute-done.4), channel_id=1, source_target_pairs={{0,32},{32,64},{64,96},{96,128},{128,160},{160,192},{192,224},{224... | collective-permute-start | bytes 159752 | tf_op jit(solution)/shard_map/ppermute | solution.py:107
  27.4 4.8 %collective-permute-start.12 = (bf16[16,1664]{1,0:T(8,128)(2,1)S(1)}, bf16[16,1664]{1,0:T(8,128)(2,1)S(1)}, u32[]{:S(2)}, u32[]{:S(2)}) collective-permute-start(bf16[16,1664]{1,0:T(8,128)(2,1)S(1)} %collective-permute-done.11), channel_id=1, source_target_pairs={{0,480},{32,0},{64,32},{96,64},{128,96},{160,128},{192,160},{224,1... | collective-permute-start | bytes 159752 | tf_op jit(solution)/shard_map/ppermute | solution.py:109
  31.9 4.8 %collective-permute-start.6 = (bf16[16,1664]{1,0:T(8,128)(2,1)S(1)}, bf16[16,1664]{1,0:T(8,128)(2,1)S(1)}, u32[]{:S(2)}, u32[]{:S(2)}) collective-permute-start(bf16[16,1664]{1,0:T(8,128)(2,1)S(1)} %collective-permute-done.5), channel_id=1, source_target_pairs={{0,32},{32,64},{64,96},{96,128},{128,160},{160,192},{192,224},{224... | collective-permute-start | bytes 159752 | tf_op jit(solution)/shard_map/ppermute | solution.py:107
  32.2 5.9 %collective-permute-start.13 = (bf16[16,1664]{1,0:T(8,128)(2,1)S(1)}, bf16[16,1664]{1,0:T(8,128)(2,1)S(1)}, u32[]{:S(2)}, u32[]{:S(2)}) collective-permute-start(bf16[16,1664]{1,0:T(8,128)(2,1)S(1)} %collective-permute-done.12), channel_id=1, source_target_pairs={{0,480},{32,0},{64,32},{96,64},{128,96},{160,128},{192,160},{224,1... | collective-permute-start | bytes 159752 | tf_op jit(solution)/shard_map/ppermute | solution.py:109
  36.6 5.5 %collective-permute-start.7 = (bf16[16,1664]{1,0:T(8,128)(2,1)S(1)}, bf16[16,1664]{1,0:T(8,128)(2,1)S(1)}, u32[]{:S(2)}, u32[]{:S(2)}) collective-permute-start(bf16[16,1664]{1,0:T(8,128)(2,1)S(1)} %collective-permute-done.6), channel_id=1, source_target_pairs={{0,32},{32,64},{64,96},{96,128},{128,160},{160,192},{192,224},{224... | collective-permute-start | bytes 159752 | tf_op jit(solution)/shard_map/ppermute | solution.py:107
  38.1 5.1 %collective-permute-start.14 = (bf16[16,1664]{1,0:T(8,128)(2,1)S(1)}, bf16[16,1664]{1,0:T(8,128)(2,1)S(1)}, u32[]{:S(2)}, u32[]{:S(2)}) collective-permute-start(bf16[16,1664]{1,0:T(8,128)(2,1)S(1)} %collective-permute-done.13), channel_id=1, source_target_pairs={{0,480},{32,0},{64,32},{96,64},{128,96},{160,128},{192,160},{224,1... | collective-permute-start | bytes 159752 | tf_op jit(solution)/shard_map/ppermute | solution.py:109
  46.0 33.5 %copy-start.4 = (f32[1664]{0:T(1024)S(1)}, f32[1664]{0:T(1024)}, u32[]{:S(2)}) copy-start(f32[1664]{0:T(1024)} %param.27) | copy-start | bytes 19972
  46.5 33.4 %copy-start.7 = (f32[1664]{0:T(1024)S(1)}, f32[1664]{0:T(1024)}, u32[]{:S(2)}) copy-start(f32[1664]{0:T(1024)} %param.29) | copy-start | bytes 19972
  46.5 33.4 %copy-start.8 = (f32[1664]{0:T(1024)S(1)}, f32[1664]{0:T(1024)}, u32[]{:S(2)}) copy-start(f32[1664]{0:T(1024)} %param.28) | copy-start | bytes 19972
  46.5 50.3 %copy-start.11 = (bf16[1664,256]{1,0:T(8,128)(2,1)S(1)}, bf16[1664,256]{1,0:T(8,128)(2,1)}, u32[]{:S(2)}) copy-start(bf16[1664,256]{1,0:T(8,128)(2,1)} %param.30) | copy-start | bytes 2555908
  46.5 50.3 %copy-start.14 = (f32[256]{0:T(256)S(1)}, f32[256]{0:T(256)}, u32[]{:S(2)}) copy-start(f32[256]{0:T(256)} %param.31) | copy-start | bytes 3076
  99.3 29.2 %all-to-all-start.1 = ((bf16[16,16,1664]{2,1,0:T(8,128)(2,1)}), bf16[16,16,1664]{2,1,0:T(8,128)(2,1)S(1)}, u32[]{:S(2)}, u32[]{:S(2)}) async-start(bf16[16,16,1664]{2,1,0:T(8,128)(2,1)} %bitcast.16), calls=%async_computation.1 | async-start | bytes 1703936 | tf_op jit(solution)/shard_map/all_to_all | solution.py:50
  128.7 17.2 %copy-start.9 = (f32[104]{0:T(128)S(1)}, f32[104]{0:T(128)}, u32[]{:S(2)}) copy-start(f32[104]{0:T(128)} %param.35) | copy-start | bytes 1252
  (9 other events, 27.2 us)
